TPU v7x, 256 devices: a whole 4x4x8 slice. The times are simulated.
256 devices in a mesh: segment: 2 (over core), ctx: 64 (over x, z, y_hi), tp: 2 (over y_lo).
Axes of the slice: x: 4, y: 4 (y_hi: 2, y_lo: 2; y = y_hi * 2 + y_lo), z: 8, core: 2. Of those that a mesh axis runs over, the one named last changes fastest.
Arguments:
- queries: bfloat16 [8192, 32, 128], P('ctx', 'tp'), may hold values from -14 to 14
- keys: bfloat16 [8192, 8, 128], P('ctx', 'tp'), may hold values from -10 to 10
- values: bfloat16 [8192, 8, 128], P('ctx', 'tp'), may hold values from -6 to 6
- layer_in: bfloat16 [8192, 4096], P('ctx', 'tp'), may hold values from -6 to 6
- w_bc: bfloat16 [1, 4096, 1024], P(None, 'tp'), may hold values from -0.09375 to 0.09375
- w_dt: bfloat16 [1, 4096, 64], P(None, 'tp'), may hold values from -0.09375 to 0.09375
- dt_bias: float32 [1, 64], P(None, 'tp'), may hold values from -1 to 1
- decay_rate: float32 [1, 64], P(None, 'tp'), may hold values from 1.2207031e-05 to 0.06
- skip_gain: float32 [1, 64], P(None, 'tp'), may hold values from 0.5 to 2
- out_gain: float32 [1, 64, 64], P(None, 'tp'), may hold values from 0.5 to 1.5
Outputs:
- section_out: bfloat16 [2, 8192, 4096], P('segment', 'ctx', 'tp')
All inputs are finite; a program needn't handle non-finite values.
Results may differ from a plain program's by a relative error of at most 0.002.
Values may be sent and summed in bfloat16 or wider, within the bound.
No kernel may reach another device: no remote copies, remote signals or barrier semaphores. Data moves between devices by JAX's collectives and lax.ppermute only.
A program may use at most 256 MiB of HBM per device.

v0:
```python
import math
import jax
import jax.numpy as jnp
from jax import lax
from jax.sharding import PartitionSpec as P

GROUPS = 4
STATE = 128
EPSILON = 1e-05


def prefix(part, axis, combine, identity):
    place = lax.axis_index(axis)
    gathered = jax.tree.map(lambda a: lax.all_gather(a, axis), part)
    state = jax.tree.map(lambda a, e: jnp.zeros_like(a) + jnp.asarray(e, a.dtype), part, identity)

    def one(turn, state):
        return combine(
            state, jax.tree.map(lambda a: lax.dynamic_index_in_dim(a, turn, 0, False), gathered)
        )

    return lax.fori_loop(0, place, one, state)


def swapped(value, axis, distance):
    mask = 2**distance
    pairs = [(source, source ^ mask) for source in range(lax.axis_size(axis))]
    return lax.ppermute(value, axis, pairs)


def span_terms(normed, b_rows, c_rows, step_sizes, rate_row, skip_row):
    count_rows, head_count, head_width = normed.shape
    group_count = b_rows.shape[1]
    per_group = head_count // group_count
    state_root = math.sqrt(b_rows.shape[2])
    log_decay = jnp.cumsum(-step_sizes * rate_row[None, :], axis=0)
    lower_mask = jnp.arange(count_rows)[:, None] >= jnp.arange(count_rows)[None, :]
    intersection = (
        jnp.einsum("tgn,sgn->gts", c_rows, b_rows, precision=lax.Precision.HIGHEST) / state_root
    )
    log_gaps = log_decay.T[:, :, None] - log_decay.T[:, None, :]
    decays = jnp.where(lower_mask[None], jnp.exp(jnp.where(lower_mask[None], log_gaps, 0.0)), 0.0)
    mixing = (
        decays.reshape(group_count, per_group, count_rows, count_rows)
        * intersection[:, None]
        * step_sizes.T.reshape(group_count, per_group, 1, count_rows)
    )
    grouped = normed.reshape(count_rows, group_count, per_group, head_width)
    local_part = jnp.einsum(
        "gkts,sgkp->tgkp", mixing, grouped, precision=lax.Precision.HIGHEST
    ).reshape(count_rows, head_count, head_width)
    tail_weight = jnp.exp(log_decay[-1][None, :] - log_decay) * step_sizes
    weighted = (normed * tail_weight[:, :, None]).reshape(
        count_rows, group_count, per_group, head_width
    )
    ending = jnp.einsum(
        "sgkp,sgn->gkpn", weighted, b_rows, precision=lax.Precision.HIGHEST
    ).reshape(head_count, head_width, b_rows.shape[2])
    return (
        log_decay,
        local_part + skip_row[None, :, None] * normed,
        ending,
        jnp.exp(log_decay[-1]),
    )


def span_inflow(log_decay, c_rows, state_in):
    count_rows, group_count, state_n = c_rows.shape
    head_count, head_width = (state_in.shape[0], state_in.shape[1])
    per_group = head_count // group_count
    state_root = math.sqrt(state_n)
    inflow = jnp.einsum(
        "tgn,gkpn->tgkp",
        c_rows,
        state_in.reshape(group_count, per_group, head_width, state_n),
        precision=lax.Precision.HIGHEST,
    )
    return (
        jnp.exp(log_decay)[:, :, None]
        * inflow.reshape(count_rows, head_count, head_width)
        / state_root
    )


def merge_states(earlier, later):
    return (earlier[0] * later[0], later[0][:, None, None] * earlier[1] + later[1])


def body(queries, keys, values, layer_in, w_bc, w_dt, dt_bias, decay_rate, skip_gain, out_gain):
    segment_index = lax.axis_index("segment")
    attention_on = segment_index == 0
    state_on = jnp.logical_not(attention_on)
    row_count, q_heads, head_width = queries.shape
    kv_heads = keys.shape[1]
    group_size = q_heads // kv_heads
    score_scale = 1.0 / math.sqrt(head_width)
    first_row = lax.axis_index("ctx") * row_count
    last_row = first_row + row_count - 1
    query_place = first_row + jnp.arange(row_count, dtype=jnp.int32)
    grouped = queries.reshape(row_count, kv_heads, group_size, head_width).transpose(1, 2, 0, 3)

    def add_block(carried, key_block, value_block, key_start):
        row_top, row_total, row_sum = carried
        scores = (
            jnp.einsum("kgqd,skd->kgqs", grouped, key_block, preferred_element_type=jnp.float32)
            * score_scale
        )
        key_place = key_start + jnp.arange(key_block.shape[0], dtype=jnp.int32)
        allowed = (query_place[:, None] >= key_place[None, :])[None, None]
        masked = jnp.where(allowed, scores, -1e30)
        new_top = jnp.maximum(row_top, jnp.max(masked, axis=3))
        raw_weight = jnp.where(allowed, jnp.exp(masked - new_top[..., None]), 0.0)
        factor = jnp.exp(row_top - new_top)
        new_total = row_total * factor + jnp.sum(raw_weight, axis=3)
        block_sum = jnp.einsum(
            "kgqs,skd->kgqd",
            raw_weight.astype(jnp.bfloat16),
            value_block,
            preferred_element_type=jnp.float32,
        )
        return (new_top, new_total, row_sum * factor[..., None] + block_sum)

    initial = (
        jnp.full((kv_heads, group_size, row_count), -1e30, jnp.float32),
        jnp.zeros((kv_heads, group_size, row_count), jnp.float32),
        jnp.zeros((kv_heads, group_size, row_count, head_width), jnp.float32),
    )
    key_piece = lax.all_gather(keys, "ctx", axis=0, tiled=True)
    value_piece = lax.all_gather(values, "ctx", axis=0, tiled=True)
    key_count = key_piece.shape[0]
    block_size = math.gcd(key_count, 1024)

    def run_all(inner_state):

        def one_step(block_index, loop_state):
            block_start = block_index * block_size
            key_block = lax.dynamic_slice_in_dim(key_piece, block_start, block_size, 0)
            value_block = lax.dynamic_slice_in_dim(value_piece, block_start, block_size, 0)
            return add_block(loop_state, key_block, value_block, block_start)

        return lax.fori_loop(0, key_count // block_size, one_step, inner_state)

    wanted = jnp.logical_and(attention_on, jnp.int32(0) <= last_row)
    row_top, row_total, row_sum = lax.cond(wanted, run_all, lambda kept_state: kept_state, initial)
    safe_total = jnp.where(attention_on, row_total, 1.0)
    mixed_out = row_sum / safe_total[..., None]
    attended = (
        mixed_out.transpose(2, 0, 1, 3)
        .reshape(row_count, q_heads * head_width)
        .astype(jnp.bfloat16)
    )
    current = layer_in
    channel_count = current.shape[1]
    heads_dev = dt_bias.shape[1]
    state_width = channel_count // heads_dev
    groups_dev = GROUPS // lax.axis_size("tp")
    wide_rows = current.astype(jnp.float32)
    part_bc = jnp.dot(current, w_bc[0], preferred_element_type=jnp.float32)
    part_dt = jnp.dot(current, w_dt[0], preferred_element_type=jnp.float32)
    part_sq = jnp.sum(wide_rows * wide_rows, axis=1)
    sum_bc, sum_dt, sum_sq = lax.psum((part_bc, part_dt, part_sq), "tp")
    inv_rms = lax.rsqrt(sum_sq / (channel_count * lax.axis_size("tp")) + EPSILON)
    normed = (wide_rows * inv_rms[:, None]).reshape(row_count, heads_dev, state_width)
    half_cols = GROUPS * STATE
    b_all = sum_bc[:, :half_cols].reshape(row_count, GROUPS, STATE)
    c_all = sum_bc[:, half_cols:].reshape(row_count, GROUPS, STATE)
    group_start = lax.axis_index("tp") * groups_dev
    b_rows = lax.dynamic_slice_in_dim(b_all, group_start, groups_dev, 1) * inv_rms[:, None, None]
    c_rows = lax.dynamic_slice_in_dim(c_all, group_start, groups_dev, 1) * inv_rms[:, None, None]
    own_dt = lax.dynamic_slice_in_dim(sum_dt, lax.axis_index("tp") * heads_dev, heads_dev, 1)
    step_sizes = jax.nn.softplus(own_dt * inv_rms[:, None] + dt_bias[0][None, :])

    def compute_terms(given):
        return span_terms(given[0], given[1], given[2], given[3], decay_rate[0], skip_gain[0])

    def empty_terms(given):
        return (
            jnp.zeros((row_count, heads_dev), jnp.float32),
            jnp.zeros((row_count, heads_dev, state_width), jnp.float32),
            jnp.zeros((heads_dev, state_width, STATE), jnp.float32),
            jnp.zeros((heads_dev,), jnp.float32),
        )

    log_decay, local_part, ending, span_decay = lax.cond(
        state_on, compute_terms, empty_terms, (normed, b_rows, c_rows, step_sizes)
    )
    decay_in, state_in = prefix(
        (span_decay, ending),
        "ctx",
        merge_states,
        (jnp.ones_like(span_decay), jnp.zeros_like(ending)),
    )
    mixed_out = local_part + span_inflow(log_decay, c_rows, state_in)
    power = jnp.mean(mixed_out * mixed_out, axis=2, keepdims=True)
    result = wide_rows.reshape(row_count, heads_dev, state_width) + out_gain[0][
        None
    ] * mixed_out * lax.rsqrt(power + EPSILON)
    current = result.reshape(row_count, channel_count).astype(jnp.bfloat16)
    result = jnp.where(attention_on, attended, current)
    incoming = swapped(result, "segment", 0)
    return incoming[None]


def solution(mesh):
    in_specs = (
        P("ctx", "tp", None),
        P("ctx", "tp", None),
        P("ctx", "tp", None),
        P("ctx", "tp"),
        P(None, "tp", None),
        P(None, "tp", None),
        P(None, "tp"),
        P(None, "tp"),
        P(None, "tp"),
        P(None, "tp", None),
    )
    out_specs = P("segment", "ctx", "tp")
    return jax.shard_map(body, mesh=mesh, in_specs=in_specs, out_specs=out_specs, check_vma=False)
```

profile of v0, /device:TPU:255, one launch (start us, length us, event | category | flops | bytes accessed | tf_op | source)
XLA Modules:
  0.0 1027.0 jit_solution(16598531643501486196)
XLA Ops:
  7.4 3.9 fusion.43
  11.4 1.6 copy.52
  13.1 1.6 copy.54
  16.7 5.7 all-reduce.1
  22.5 28.7 %all-reduce.4.cloned.1.call-done = f32[128,1024]{1,0:T(8,128)} async-done(((f32[128,1024]{1,0:T(8,128)}), f32[128,1024]{1,0:T(8,128)}) %all-reduce.4.cloned.1.call-update) | async-done | bytes 524304 | tf_op jit(solution)/shard_map/psum | solution.py:161
  53.1 19.6 %conditional.3 = (f32[128,32]{1,0:T(8,128)}, f32[128,32,64]{0,2,1:T(8,128)S(1)}, f32[32,64,128]{2,1,0:T(8,128)}, f32[32]{0:T(128)}) conditional(s32[]{:T(128)} %convert_element_type.36, () %tuple.55, (s32[]{:T(128)}, f32[128,64]{0,1:T(8,128)S(1)}, f32[128]{0:T(128)S(1)}, f32[1,32]{1,0:T(1,128)S(1)}, f32[1,32]{1,0:T(1,128)S(1)}, ...), branch_computations={%region_10.11_spmd, %region_11.13_spmd} | conditional | flops 860024832 | bytes 13620502 | solution.py:184
  54.8 1.6 exponential_multiply_fusion
  56.4 1.5 copy.45
  61.5 5.2 fusion
  68.4 3.1 fusion.8
  76.8 152.8 %all-reduce = f32[2048]{0:T(1024)S(1)} all-reduce(f32[2048]{0:T(1024)S(1)} %dynamic-update-slice), channel_id=2, replica_groups=mesh['segment'=2,'ctx'=64,'tp'=2] {'ctx'}, use_global_device_ids=true, to_apply=%add | all-reduce | flops 2048 | bytes 16384
  231.2 72.4 %all-gather.8.cloned.1.call-done = bf16[8192,4,128]{2,0,1:T(8,128)(2,1)} async-done(((bf16[128,4,128]{2,0,1:T(8,128)(2,1)}), bf16[8192,4,128]{2,0,1:T(8,128)(2,1)}) %all-gather.8.cloned.1.call-update) | async-done | bytes 8388624 | tf_op jit(solution)/shard_map/all_gather | solution.py:129
  303.6 1.7 conditional.2
  305.3 1.6 fusion.47
  307.9 568.6 %all-gather.10.cloned.1.call-done = f32[2048,64,128]{2,1,0:T(8,128)} async-done(((f32[32,64,128]{2,1,0:T(8,128)}), f32[2048,64,128]{2,1,0:T(8,128)}) %all-gather.10.cloned.1.call-update) | async-done | bytes 67108880 | tf_op jit(solution)/shard_map/all_gather | solution.py:14
  876.6 136.0 %while.30 = (s32[]{:T(128)}, f32[32,64,128]{2,1,0:T(8,128)S(1)}, s32[]{:T(128)}, f32[64,32]{1,0:T(8,128)}, f32[64,32,64,128]{3,2,1,0:T(8,128)}, /*index=5*/s32[]{:T(128)}, s32[]{:T(128)}, s32[]{:T(128)}) while((s32[]{:T(128)}, f32[32,64,128]{2,1,0:T(8,128)S(1)}, s32[]{:T(128)}, f32[64,32]{1,0:T(8,128)}, f32[64,32,64,128]{3,2,1,0:T(8,128)}, ...), condition=%wide.region_14.15_spmd, body=%wide.region_13.14_spmd.sunk | while | flops 524293 | bytes 3146239 | solution.py:22
  877.3 1.4 bitcast_add_fusion.3
  879.5 1.4 bitcast_add_fusion.3
  881.7 1.4 bitcast_add_fusion.3
  883.8 1.4 bitcast_add_fusion.3
  886.0 1.4 bitcast_add_fusion.3
  888.1 1.4 bitcast_add_fusion.3
  890.3 1.4 bitcast_add_fusion.3
  892.4 1.4 bitcast_add_fusion.3
  894.6 1.4 bitcast_add_fusion.3
  896.7 1.4 bitcast_add_fusion.3
  898.9 1.4 bitcast_add_fusion.3
  901.1 1.4 bitcast_add_fusion.3
  903.2 1.4 bitcast_add_fusion.3
  905.4 1.4 bitcast_add_fusion.3
  911.8 1.4 bitcast_add_fusion.3
  920.5 1.4 bitcast_add_fusion.3
  922.7 1.4 bitcast_add_fusion.3
  929.2 1.4 bitcast_add_fusion.3
  935.7 1.4 bitcast_add_fusion.3
  940.0 1.4 bitcast_add_fusion.3
  944.3 1.4 bitcast_add_fusion.3
  959.4 1.4 bitcast_add_fusion.3
  963.7 1.4 bitcast_add_fusion.3
  970.2 1.4 bitcast_add_fusion.3
  974.5 1.4 bitcast_add_fusion.3
  983.1 1.4 bitcast_add_fusion.3
  991.7 1.4 bitcast_add_fusion.3
  1004.7 1.4 bitcast_add_fusion.3
  1006.9 1.4 bitcast_add_fusion.3
  1009.0 1.4 bitcast_add_fusion.3
  1015.3 1.6 collective-permute-start
  1016.8 1.5 collective-permute-done
  (162 shorter events, 114.4 us)
Async XLA Ops:
  7.4 9.1 copy-start
  7.4 9.1 copy-start.2
  7.4 45.7 %copy-start.6 = (f32[1,32]{1,0:T(1,128)S(1)}, f32[1,32]{1,0:T(1,128)}, u32[]{:S(2)}) copy-start(f32[1,32]{1,0:T(1,128)} %param.24) | copy-start | bytes 388
  7.4 45.7 %copy-start.7 = (f32[1,32]{1,0:T(1,128)S(1)}, f32[1,32]{1,0:T(1,128)}, u32[]{:S(2)}) copy-start(f32[1,32]{1,0:T(1,128)} %param.25) | copy-start | bytes 388
  7.4 43.8 %all-reduce.4.cloned.1.call-start = ((), (), s32[]{:S(2)}) async-start(), calls=%async_computation.2 | async-start | bytes 1048576 | tf_op jit(solution)/shard_map/psum | solution.py:161
  11.4 219.8 %all-gather.6.cloned.1.call-start = ((), (), s32[]{:S(2)}) async-start(), calls=%async_computation | async-start | bytes 8519680 | tf_op jit(solution)/shard_map/all_gather | solution.py:128
  13.0 290.6 %all-gather.8.cloned.1.call-start = ((), (), s32[]{:S(2)}) async-start(), calls=%async_computation.1 | async-start | bytes 8519680 | tf_op jit(solution)/shard_map/all_gather | solution.py:129
  14.7 861.8 %all-gather.10.cloned.1.call-start = ((), (), s32[]{:S(2)}) async-start(), calls=%async_computation.3 | async-start | bytes 68157440 | tf_op jit(solution)/shard_map/all_gather | solution.py:14
  53.1 4.9 copy-start.5
  59.9 6.8 copy-start.4
  1012.6 2.5 copy-start.3
  1015.3 3.1 collective-permute-start
Sparse Core Ops, SparseCore 0:
  11.5 39.6 all-reduce.3
Sparse Core Ops, SparseCore 1:
  15.4 142.0 all-gather.5
  160.9 142.7 all-gather.7
  307.0 569.5 all-gather.9
where the time goes:
time: 1030 us
  waiting for transfers between devices  671 us (65%)
  blocking collectives  158 us (15%)
  other arithmetic  98.3 us (10%)
  local copies, waits for them, and re-layouts  64.2 us (6%)
  between operations  15.9 us (2%)
  matrix products  14.9 us (1%)
    all_gather x1, waiting for transfers between devices, prefix(): gathered = jax.tree.map(lambda a: lax.all_gather(a, axis), part)  569 us
    unnamed x1, blocking collectives  153 us
    add x63, other arithmetic, merge_states(): later[0][:, None, None] * earlier[1] + later[1]  90.7 us
    all_gather x1, waiting for transfers between devices, body(): value_piece = lax.all_gather(values, 'ctx', axis=0, tiled=True)  72.4 us
    mul x63, local copies, waits for them, and re-layouts, merge_states(): later[0][:, None, None] * earlier[1] + later[1]  43.3 us
    psum x1, waiting for transfers between devices, body(): sum_bc, sum_dt, sum_sq = lax.psum((part_bc, part_dt, part_sq), 'tp')  28.7 us
  transfers between devices with their start and end apart: 5, of which 4 were waited for; matrix products, arithmetic and copies ran while one was open for 3% of the time, Pallas kernels for 0%

commit v1 on v0

--- a/solution.py
+++ b/solution.py
@@ -126,7 +126,9 @@
         jnp.zeros((kv_heads, group_size, row_count, head_width), jnp.float32),
     )
     key_piece = lax.all_gather(keys, "ctx", axis=0, tiled=True)
-    value_piece = lax.all_gather(values, "ctx", axis=0, tiled=True)
+    value_piece = jnp.concatenate(
+        lax.all_to_all(jnp.stack(lax.axis_size("ctx") * [values], axis=0), "ctx", 0, 0), axis=0
+    )
     key_count = key_piece.shape[0]
     block_size = math.gcd(key_count, 1024)
 

time: 1030 us -> 992 us (0.963)
  waiting for transfers between devices: 671 us -> 404 us
  blocking collectives: 158 us -> 370 us
  starting transfers between devices: 1.72 us -> 14 us
    unnamed x1, blocking collectives: 153 us -> 364 us
    all_gather x1, waiting for transfers between devices: 569 us -> 372 us  [prefix(): gathered = jax.tree.map(lambda a: lax.all_gather(a, axis), part)]
    all_gather x1 -> x0, waiting for transfers between devices: 72.4 us -> none  [body(): value_piece = lax.all_gather(values, 'ctx', axis=0, tiled=True)]
    all_to_all x0 -> x1, starting transfers between devices: none -> 12.4 us  [body(): lax.all_to_all(jnp.stack(lax.axis_size('ctx') * [values], axis=0), 'ctx',...]
  transfers between devices with their start and end apart: 5 -> 5, of which waited for: 4 -> 3; matrix products, arithmetic and copies ran while one was open for 3% -> 4% of each run, Pallas kernels for 0% -> 0%
where the time goes in v1:
time: 992 us; the launch traced here: 986 us
  waiting for transfers between devices  404 us (41%)
  blocking collectives  370 us (37%)
  other arithmetic  98.3 us (10%)
  local copies, waits for them, and re-layouts  67.2 us (7%)
  between operations  15.8 us (2%)
  matrix products  14.9 us (2%)
  starting transfers between devices  14 us (1%)
    all_gather x1, waiting for transfers between devices, prefix(): gathered = jax.tree.map(lambda a: lax.all_gather(a, axis), part)  372 us
    unnamed x1, blocking collectives  364 us
    add x63, other arithmetic, merge_states(): later[0][:, None, None] * earlier[1] + later[1]  90.7 us
    mul x63, local copies, waits for them, and re-layouts, merge_states(): later[0][:, None, None] * earlier[1] + later[1]  43.4 us
    psum x1, waiting for transfers between devices, body(): sum_bc, sum_dt, sum_sq = lax.psum((part_bc, part_dt, part_sq), 'tp')  30.4 us
  transfers between devices with their start and end apart: 5, of which 3 were waited for; matrix products, arithmetic and copies ran while one was open for 4% of the time, Pallas kernels for 0%

profile of v1, /device:TPU:255, one launch (start us, length us, event | category | flops | bytes accessed | tf_op | source)
XLA Modules:
  0.0 986.4 jit_solution(7200397149791931803)
XLA Ops:
  7.4 3.9 fusion.43
  11.4 1.6 copy.53
  15.1 5.7 all-reduce.1
  20.8 30.4 %all-reduce.4.cloned.1.call-done = f32[128,1024]{1,0:T(8,128)} async-done(((f32[128,1024]{1,0:T(8,128)}), f32[128,1024]{1,0:T(8,128)}) %all-reduce.4.cloned.1.call-update) | async-done | bytes 524304 | tf_op jit(solution)/shard_map/psum | solution.py:163
  53.1 19.6 %conditional.3 = (f32[128,32]{1,0:T(8,128)}, f32[128,32,64]{0,2,1:T(8,128)S(1)}, f32[32,64,128]{2,1,0:T(8,128)}, f32[32]{0:T(128)}) conditional(s32[]{:T(128)} %convert_element_type.36, () %tuple.55, (s32[]{:T(128)}, f32[128,64]{0,1:T(8,128)S(1)}, f32[128]{0:T(128)S(1)}, f32[1,32]{1,0:T(1,128)S(1)}, f32[1,32]{1,0:T(1,128)S(1)}, ...), branch_computations={%region_10.11_spmd, %region_11.13_spmd} | conditional | flops 860024832 | bytes 13620502 | solution.py:186
  54.8 1.6 exponential_multiply_fusion
  56.4 1.5 copy.45
  61.5 5.2 fusion
  68.4 3.0 fusion.8
  73.6 5.3 stack.2
  79.0 12.4 %all-to-all-start = ((bf16[64,128,4,128]{3,1,2,0:T(8,128)(2,1)}), bf16[64,128,4,128]{3,1,2,0:T(8,128)(2,1)}, u32[]{:S(2)}, u32[]{:S(2)}) async-start(bf16[64,128,4,128]{3,1,2,0:T(8,128)(2,1)} %stack.2), calls=%async_computation | async-start | bytes 16777216 | tf_op jit(solution)/shard_map/all_to_all | solution.py:130
  93.7 364.1 %all-reduce = f32[2048]{0:T(1024)S(1)} all-reduce(f32[2048]{0:T(1024)S(1)} %dynamic-update-slice), channel_id=2, replica_groups=mesh['segment'=2,'ctx'=64,'tp'=2] {'ctx'}, use_global_device_ids=true, to_apply=%add | all-reduce | flops 2048 | bytes 16384
  459.5 1.7 conditional.2
  461.2 1.6 fusion.47
  463.8 372.3 %all-gather.7.cloned.1.call-done = f32[2048,64,128]{2,1,0:T(8,128)} async-done(((f32[32,64,128]{2,1,0:T(8,128)}), f32[2048,64,128]{2,1,0:T(8,128)}) %all-gather.7.cloned.1.call-update) | async-done | bytes 67108880 | tf_op jit(solution)/shard_map/all_gather | solution.py:14
  836.2 136.1 %while.30 = (s32[]{:T(128)}, f32[32,64,128]{2,1,0:T(8,128)S(1)}, s32[]{:T(128)}, f32[64,32]{1,0:T(8,128)}, f32[64,32,64,128]{3,2,1,0:T(8,128)}, /*index=5*/s32[]{:T(128)}, s32[]{:T(128)}, s32[]{:T(128)}) while((s32[]{:T(128)}, f32[32,64,128]{2,1,0:T(8,128)S(1)}, s32[]{:T(128)}, f32[64,32]{1,0:T(8,128)}, f32[64,32,64,128]{3,2,1,0:T(8,128)}, ...), condition=%wide.region_14.15_spmd, body=%wide.region_13.14_spmd.sunk | while | flops 524293 | bytes 3146239 | solution.py:22
  836.9 1.4 bitcast_add_fusion.3
  845.5 1.4 bitcast_add_fusion.3
  847.7 1.4 bitcast_add_fusion.3
  849.9 1.4 bitcast_add_fusion.3
  858.5 1.4 bitcast_add_fusion.3
  860.7 1.4 bitcast_add_fusion.3
  869.3 1.4 bitcast_add_fusion.3
  871.5 1.4 bitcast_add_fusion.3
  882.3 1.4 bitcast_add_fusion.3
  884.4 1.4 bitcast_add_fusion.3
  893.0 1.4 bitcast_add_fusion.3
  897.4 1.4 bitcast_add_fusion.3
  901.7 1.4 bitcast_add_fusion.3
  908.1 1.4 bitcast_add_fusion.3
  910.3 1.4 bitcast_add_fusion.3
  912.4 1.4 bitcast_add_fusion.3
  923.2 1.4 bitcast_add_fusion.3
  925.4 1.4 bitcast_add_fusion.3
  936.2 1.4 bitcast_add_fusion.3
  938.4 1.4 bitcast_add_fusion.3
  944.9 1.4 bitcast_add_fusion.3
  951.4 1.4 bitcast_add_fusion.3
  955.7 1.4 bitcast_add_fusion.3
  957.8 1.4 bitcast_add_fusion.3
  960.0 1.4 bitcast_add_fusion.3
  962.2 1.4 bitcast_add_fusion.3
  964.3 1.4 bitcast_add_fusion.3
  966.5 1.4 bitcast_add_fusion.3
  968.6 1.4 bitcast_add_fusion.3
  970.8 1.4 bitcast_add_fusion.3
  974.9 1.6 collective-permute-start
  976.4 1.5 collective-permute-done
  (166 shorter events, 113.6 us)
Async XLA Ops:
  7.4 7.4 copy-start
  7.4 7.4 copy-start.2
  7.4 45.7 %copy-start.7 = (f32[1,32]{1,0:T(1,128)S(1)}, f32[1,32]{1,0:T(1,128)}, u32[]{:S(2)}) copy-start(f32[1,32]{1,0:T(1,128)} %param.24) | copy-start | bytes 388
  7.4 45.7 %copy-start.8 = (f32[1,32]{1,0:T(1,128)S(1)}, f32[1,32]{1,0:T(1,128)}, u32[]{:S(2)}) copy-start(f32[1,32]{1,0:T(1,128)} %param.25) | copy-start | bytes 388
  7.4 43.8 %all-reduce.4.cloned.1.call-start = ((), (), s32[]{:S(2)}) async-start(), calls=%async_computation.2 | async-start | bytes 1048576 | tf_op jit(solution)/shard_map/psum | solution.py:163
  11.4 448.1 %all-gather.5.cloned.1.call-start = ((), (), s32[]{:S(2)}) async-start(), calls=%async_computation.1 | async-start | bytes 8519680 | tf_op jit(solution)/shard_map/all_gather | solution.py:128
  13.0 823.0 %all-gather.7.cloned.1.call-start = ((), (), s32[]{:S(2)}) async-start(), calls=%async_computation.3 | async-start | bytes 68157440 | tf_op jit(solution)/shard_map/all_gather | solution.py:14
  53.1 4.9 copy-start.6
  60.0 6.8 copy-start.4
  79.0 12.4 %copy-start.5 = (bf16[128,16,128]{2,1,0:T(8,128)(2,1)S(1)}, bf16[128,16,128]{2,1,0:T(8,128)(2,1)}, u32[]{:S(2)}) copy-start(bf16[128,16,128]{2,1,0:T(8,128)(2,1)} %param.18) | copy-start | bytes 1572868
  79.0 12.5 %copy-start.9 = (u32[256]{0:T(256)S(1)}, u32[256]{0:T(256)}, u32[]{:S(2)}) copy-start(u32[256]{0:T(256)} %constant.160) | copy-start | bytes 3076
  79.0 380.5 %all-to-all-start = ((bf16[64,128,4,128]{3,1,2,0:T(8,128)(2,1)}), bf16[64,128,4,128]{3,1,2,0:T(8,128)(2,1)}, u32[]{:S(2)}, u32[]{:S(2)}) async-start(bf16[64,128,4,128]{3,1,2,0:T(8,128)(2,1)} %stack.2), calls=%async_computation | async-start | bytes 16777216 | tf_op jit(solution)/shard_map/all_to_all | solution.py:130
  972.3 2.5 copy-start.3
  974.9 3.1 collective-permute-start
Sparse Core Ops, SparseCore 0:
  11.5 39.6 all-reduce.3
Sparse Core Ops, SparseCore 1:
  15.4 209.4 all-gather.4
  228.2 607.8 all-gather.6
